TPU v7x, 256 devices: a whole 4x4x8 slice. The times are simulated.
256 devices in a mesh: dp: 32 (over z, x), tensor: 8 (over y, core).
Axes of the slice: x: 4, y: 4, z: 8, core: 2. Of those that a mesh axis runs over, the one named last changes fastest.
Arguments:
- gradients: float32 [32, 2368, 1024], P('dp', None, 'tensor'), may hold values from -96 to 96
- weights: float32 [2368, 1024], P(None, 'tensor'), may hold values from -64 to 64
- first_moment: float32 [2368, 1024], P(None, 'tensor'), may hold values from -64 to 64
- second_moment: float32 [2368, 1024], P(None, 'tensor'), may hold values from 0.05 to 2
Outputs:
- weights_new: float32 [2368, 1024], P(None, 'tensor')
- first_new: float32 [2368, 1024], P(None, 'tensor')
- second_new: float32 [2368, 1024], P(None, 'tensor')
- copies: bfloat16 [2368, 1024], replicated
- ratios: float32 [4], replicated
All inputs are finite; a program needn't handle non-finite values.
Results may differ from a plain program's by a relative error of at most 0.0004.
Values may be sent and summed in bfloat16 or wider, within the bound.
No kernel may reach another device: no remote copies, remote signals or barrier semaphores. Data moves between devices by JAX's collectives and lax.ppermute only.
A program may use at most 64 MiB of HBM per device.

v0:
```python
import jax
import jax.numpy as jnp
import numpy as np
from jax import lax
from jax.sharding import Mesh
from jax.sharding import PartitionSpec as P

D = 1024
HID = 1342
beta_one = 0.9
beta_two = 0.999
correct_one = 1.0 - 0.9**20
correct_two = 1.0 - 0.999**20
epsilon = 1e-06
learn_rate = 0.01
decay_rate = 0.01
DP = ("z", "x")
TN = ("y", "core")


def group_table(row_count):
    row_ids = lax.broadcasted_iota(jnp.int32, (row_count, 4), 0)
    which = lax.broadcasted_iota(jnp.int32, (row_count, 4), 1)
    group = jnp.where(row_ids < D, 0, jnp.where(row_ids < D + HID, 1, row_ids - D - HID + 2))
    return (group == which).astype(jnp.float32)


def group_squares(values, seg_table):
    row_sums = jnp.sum(values * values, axis=1)
    return jnp.dot(row_sums, seg_table, precision=lax.Precision.HIGHEST)


def adam_part(grad, weights, first_moment, second_moment, seg_table):
    first_new = beta_one * first_moment + (1.0 - beta_one) * grad
    second_new = beta_two * second_moment + (1.0 - beta_two) * grad * grad
    decay = decay_rate * (seg_table[:, 0] + seg_table[:, 1])
    update = (
        first_new / correct_one / (jnp.sqrt(second_new / correct_two) + epsilon)
        + decay[:, None] * weights
    )
    return (first_new, second_new, update)


def apply_ratios(weights, update, seg_table, weight_total, step_total):
    ratios = jnp.sqrt(weight_total) / jnp.sqrt(step_total)
    row_ratio = jnp.dot(seg_table, ratios, precision=lax.Precision.HIGHEST)
    return (weights - learn_rate * row_ratio[:, None] * update, ratios)


def dp_sum(x, nz, nx):
    rows, cols = x.shape
    unit = 8 * nz * nx
    padded = -(-rows // unit) * unit
    y = jnp.pad(x, ((0, padded - rows), (0, 0)))
    y = lax.all_to_all(y.reshape(nx, padded // nx, cols), "x", 0, 0, tiled=False).sum(0)
    y = lax.all_to_all(y.reshape(nz, padded // (nx * nz), cols), "z", 0, 0, tiled=False).sum(0)
    y = lax.all_to_all(jnp.broadcast_to(y[None], (nz,) + y.shape), "z", 0, 0, tiled=False)
    y = y.reshape(padded // nx, cols)
    y = lax.all_to_all(jnp.broadcast_to(y[None], (nx,) + y.shape), "x", 0, 0, tiled=False)
    return y.reshape(padded, cols)[:rows]


def tensor_sum(v, ny, ncore):
    for axis, size in (("core", ncore), ("y", ny)):
        step = 1
        while step < size:
            v = v + lax.ppermute(v, axis, [(i, i ^ step) for i in range(size)])
            step *= 2
    return v


def make_shards(nz, nx, ny, ncore):

    def shards(gradients, weights, first_moment, second_moment):
        local_grad = gradients[0]
        row_count = weights.shape[0]
        seg_table = group_table(row_count)
        grad = dp_sum(local_grad, nz, nx) / (nz * nx)
        first_new, second_new, update = adam_part(
            grad, weights, first_moment, second_moment, seg_table
        )
        both = jnp.concatenate(
            [group_squares(weights, seg_table), group_squares(update, seg_table)]
        )
        both = tensor_sum(both, ny, ncore)
        weight_total, step_total = (both[:4], both[4:])
        weights_new, ratios = apply_ratios(weights, update, seg_table, weight_total, step_total)
        copies = lax.all_gather(weights_new.astype(jnp.bfloat16), TN, axis=1, tiled=True)
        return (weights_new, first_new, second_new, copies, ratios)

    return shards


def physical_mesh(mesh):
    devices = mesh.devices
    dp_devices = devices[:, 0]
    nx = len({d.coords[0] for d in dp_devices})
    nz = dp_devices.size // nx
    tn_devices = devices[0, :]
    ncore = len({d.core_on_chip for d in tn_devices})
    ny = tn_devices.size // ncore
    return (Mesh(devices.reshape(nz, nx, ny, ncore), ("z", "x", "y", "core")), (nz, nx, ny, ncore))


def solution(mesh):
    mesh2, sizes = physical_mesh(mesh)
    return jax.shard_map(
        make_shards(*sizes),
        mesh=mesh2,
        in_specs=(P(DP, None, TN), P(None, TN), P(None, TN), P(None, TN)),
        out_specs=(P(None, TN), P(None, TN), P(None, TN), P(), P()),
        check_vma=False,
    )
```

profile of v0, /device:TPU:1, one launch (start us, length us, event | category | flops | bytes accessed | tf_op | source)
XLA Modules:
  0.0 149.0 jit_solution(8851995358770724701)
XLA Ops:
  7.2 1.4 pad.4
  8.5 21.6 %all_to_all.20 = f32[4,640,128]{2,1,0:T(8,128)S(1)} all-to-all(f32[4,640,128]{2,1,0:T(8,128)S(1)} %bitcast.17), channel_id=1, replica_groups=mesh['z'=8,'x'=4,'y'=4,'core'=2] {'x'}, dimensions={0} | all-to-all | bytes 2621440 | tf_op jit(solution)/shard_map/all_to_all | solution.py:55
  30.2 0.1 reduce_sum.37
  30.3 18.7 %all_to_all.21 = f32[8,80,128]{2,1,0:T(8,128)S(1)} all-to-all(f32[8,80,128]{2,1,0:T(8,128)S(1)} %bitcast.19), channel_id=1, replica_groups=mesh['z'=8,'x'=4,'y'=4,'core'=2] {'z'}, dimensions={0} | all-to-all | bytes 655360 | tf_op jit(solution)/shard_map/all_to_all | solution.py:56
  49.0 12.8 %all_to_all.22 = f32[8,80,128]{2,1,0:T(8,128)S(1)} all-to-all(f32[8,80,128]{2,1,0:T(8,128)S(1)} %broadcast_in_dim.24), channel_id=1, replica_groups=mesh['z'=8,'x'=4,'y'=4,'core'=2] {'z'}, dimensions={0} | all-to-all | bytes 655360 | tf_op jit(solution)/shard_map/all_to_all | solution.py:57
  61.8 1.1 broadcast_in_dim.26
  62.9 0.0 copy-start
  62.9 3.7 %all-to-all-start.3 = ((f32[4,640,128]{2,1,0:T(8,128)}), f32[4,640,128]{2,1,0:T(8,128)S(1)}, u32[]{:S(2)}, u32[]{:S(2)}) async-start(f32[4,640,128]{2,1,0:T(8,128)} %broadcast_in_dim.26), calls=%async_computation.3 | async-start | bytes 2621440 | tf_op jit(solution)/shard_map/all_to_all | solution.py:59
  66.6 0.0 all-gather.2.cloned.1.call-start
  66.8 13.2 %all-to-all-done.3 = f32[4,640,128]{2,1,0:T(8,128)S(1)} async-done(((f32[4,640,128]{2,1,0:T(8,128)}), f32[4,640,128]{2,1,0:T(8,128)S(1)}, u32[]{:S(2)}, u32[]{:S(2)}) %all-to-all-start.3) | async-done | bytes 1310752 | tf_op jit(solution)/shard_map/all_to_all | solution.py:59
  79.9 0.0 copy-done
  79.9 4.0 %multiply_reduce_fusion = (f32[2368]{0:T(1024)S(1)}, f32[2368,128]{1,0:T(8,128)S(1)}, f32[2368,128]{1,0:T(8,128)}, f32[2368,128]{1,0:T(8,128)}, f32[2368]{0:T(1024)S(1)}) fusion(f32[2368,128]{1,0:T(8,128)S(1)} %copy-done, f32[2368]{0:T(1024)S(1)} %fusion.1, f32[2560,128]{1,0:T(8,128)S(1)} %bitcast.18, f32[2368,128]{1,0:T(8,128)} %param.6, f32[2368,128]{1,0:T(8,128)} %param.7), kind=kLoop, calls=%fused_computation.1 | loop fusion | flops 5451136 | bytes 8515328 | tf_op jit(solution)/shard_map/reduce_sum | solution.py:29
  83.9 0.1 convolution_bitcast_fusion
  84.1 0.2 convolution_bitcast_fusion.1
  84.3 0.1 pad_maximum_fusion
  84.4 5.5 %collective-permute-start = (f32[8]{0:T(128)S(1)}, f32[8]{0:T(128)S(1)}, u32[]{:S(2)}, u32[]{:S(2)}) collective-permute-start(f32[8]{0:T(128)S(1)} %pad_maximum_fusion), channel_id=1, source_target_pairs={{0,1},{1,0},{2,3},{3,2},{4,5},{5,4},{6,7},{7,6},{8,9},{9,8},{10,11... | collective-permute-start | bytes 104 | tf_op jit(solution)/shard_map/ppermute | solution.py:67
  89.9 0.8 collective-permute-done
  90.7 0.1 fusion.10
  90.8 1.3 collective-permute-start.1
  92.1 1.1 collective-permute-done.1
  93.3 2.9 %collective-permute-start.2 = (f32[8]{0:T(128)S(1)}, f32[8]{0:T(128)S(1)}, u32[]{:S(2)}, u32[]{:S(2)}) collective-permute-start(f32[8]{0:T(128)S(1)} %add.59), channel_id=1, source_target_pairs={{0,4},{2,6},{4,0},{6,2},{1,5},{3,7},{5,1},{7,3},{8,12},{10,14},{12... | collective-permute-start | bytes 104 | tf_op jit(solution)/shard_map/ppermute | solution.py:67
  96.2 1.0 collective-permute-done.2
  97.2 0.1 rsqrt_multiply_fusion
  97.3 0.0 copy-start.1
  97.3 0.2 convolution_reduce_fusion
  97.5 1.6 %fusion.3 = (bf16[2368,128]{1,0:T(8,128)(2,1)}, f32[2368,128]{1,0:T(8,128)}) fusion(f32[2368,128]{1,0:T(8,128)S(1)} %copy-done, f32[2368,128]{1,0:T(8,128)S(1)} %get-tuple-element.8, f32[2368]{0:T(1024)S(1)} %broadcast_multiply_fusion), kind=kLoop, calls=%fused_computation.20 | loop fusion | flops 909312 | bytes 4252928 | tf_op jit(solution)/shard_map/convert_element_type | solution.py:88
  99.1 0.0 copy-done.1
  99.1 0.0 all-gather.2.cloned.1.call-update
  99.1 38.0 %all-gather.2.cloned.1.call-done = bf16[2368,1024]{1,0:T(8,128)(2,1)} async-done(((bf16[2368,128]{1,0:T(8,128)(2,1)}), bf16[2368,1024]{1,0:T(8,128)(2,1)}) %all-gather.2.cloned.1.call-update) | async-done | bytes 4849680 | tf_op jit(solution)/shard_map/all_gather | solution.py:88
  137.1 5.1 %copy.10 = bf16[2368,1024]{1,0:T(8,128)(2,1)} copy(bf16[2368,1024]{1,0:T(8,128)(2,1)} %all-gather.2.cloned.1.call-done) | data formatting | bytes 9699328
  (11 shorter events, 0.2 us)
Async XLA Ops:
  62.9 17.0 %copy-start = (f32[2368,128]{1,0:T(8,128)S(1)}, f32[2368,128]{1,0:T(8,128)}, u32[]{:S(2)}) copy-start(f32[2368,128]{1,0:T(8,128)} %param.5) | copy-start | bytes 3637252
  62.9 17.0 %all-to-all-start.3 = ((f32[4,640,128]{2,1,0:T(8,128)}), f32[4,640,128]{2,1,0:T(8,128)S(1)}, u32[]{:S(2)}, u32[]{:S(2)}) async-start(f32[4,640,128]{2,1,0:T(8,128)} %broadcast_in_dim.26), calls=%async_computation.3 | async-start | bytes 2621440 | tf_op jit(solution)/shard_map/all_to_all | solution.py:59
  66.6 70.5 %all-gather.2.cloned.1.call-start = ((), (), s32[]{:S(2)}) async-start(), calls=%async_computation.4 | async-start | bytes 5455872 | tf_op jit(solution)/shard_map/all_gather | solution.py:88
  84.4 6.4 %collective-permute-start = (f32[8]{0:T(128)S(1)}, f32[8]{0:T(128)S(1)}, u32[]{:S(2)}, u32[]{:S(2)}) collective-permute-start(f32[8]{0:T(128)S(1)} %pad_maximum_fusion), channel_id=1, source_target_pairs={{0,1},{1,0},{2,3},{3,2},{4,5},{5,4},{6,7},{7,6},{8,9},{9,8},{10,11... | collective-permute-start | bytes 104 | tf_op jit(solution)/shard_map/ppermute | solution.py:67
  90.8 2.4 %collective-permute-start.1 = (f32[8]{0:T(128)S(1)}, f32[8]{0:T(128)S(1)}, u32[]{:S(2)}, u32[]{:S(2)}) collective-permute-start(f32[8]{0:T(128)S(1)} %fusion.10), channel_id=1, source_target_pairs={{0,2},{2,0},{4,6},{6,4},{1,3},{3,1},{5,7},{7,5},{8,10},{10,8},{12,... | collective-permute-start | bytes 104 | tf_op jit(solution)/shard_map/ppermute | solution.py:67
  93.3 3.9 %collective-permute-start.2 = (f32[8]{0:T(128)S(1)}, f32[8]{0:T(128)S(1)}, u32[]{:S(2)}, u32[]{:S(2)}) collective-permute-start(f32[8]{0:T(128)S(1)} %add.59), channel_id=1, source_target_pairs={{0,4},{2,6},{4,0},{6,2},{1,5},{3,7},{5,1},{7,3},{8,12},{10,14},{12... | collective-permute-start | bytes 104 | tf_op jit(solution)/shard_map/ppermute | solution.py:67
  97.3 1.8 %copy-start.1 = (f32[4]{0:T(128)}, f32[4]{0:T(128)S(1)}, u32[]{:S(2)}) copy-start(f32[4]{0:T(128)S(1)} %rsqrt_multiply_fusion) | copy-start | bytes 52
Sparse Core Ops, SparseCore 0:
  99.2 37.7 all-gather.1
where the time goes:
time: 149 us
  waiting for transfers between devices  54.1 us (36%)
  blocking collectives  53.1 us (36%)
  between operations  14.1 us (9%)
  starting transfers between devices  13.5 us (9%)
  local copies, waits for them, and re-layouts  7.68 us (5%)
  other arithmetic  6.06 us (4%)
    all_gather x1, waiting for transfers between devices, shards(): lax.all_gather(weights_new.astype(jnp.bfloat16), TN, axis=1, tiled=True)  38 us
    all_to_all x1, blocking collectives, dp_sum(): lax.all_to_all(y.reshape(nx, padded // nx, cols), 'x', 0, 0, tiled=False)  21.6 us
    all_to_all x1, blocking collectives, dp_sum(): lax.all_to_all(y.reshape(nz, padded // (nx * nz), cols), 'z', 0, 0, tiled...  18.7 us
    all_to_all x1, waiting for transfers between devices, dp_sum(): lax.all_to_all(jnp.broadcast_to(y[None], (nx,) + y.shape), 'x', 0, 0, til...  13.2 us
    all_to_all x1, blocking collectives, dp_sum(): lax.all_to_all(jnp.broadcast_to(y[None], (nz,) + y.shape), 'z', 0, 0, til...  12.8 us
    ppermute x3, starting transfers between devices, tensor_sum(): v = v + lax.ppermute(v, axis, [(i, i ^ step) for i in range(size)])  9.76 us
    unnamed x5, local copies, waits for them, and re-layouts  5.13 us
    reduce_sum x1, other arithmetic, group_squares(): row_sums = jnp.sum(values * values, axis=1)  3.96 us
  transfers between devices with their start and end apart: 5, of which 5 were waited for; matrix products, arithmetic and copies ran while one was open for 0% of the time, Pallas kernels for 0%

commit v1 on v0

--- a/solution.py
+++ b/solution.py
@@ -85,7 +85,12 @@
         both = tensor_sum(both, ny, ncore)
         weight_total, step_total = (both[:4], both[4:])
         weights_new, ratios = apply_ratios(weights, update, seg_table, weight_total, step_total)
-        copies = lax.all_gather(weights_new.astype(jnp.bfloat16), TN, axis=1, tiled=True)
+        copies = jnp.concatenate(
+            lax.all_to_all(
+                jnp.stack([weights_new.astype(jnp.bfloat16)] * lax.axis_size(TN)), TN, 0, 0
+            ),
+            axis=1,
+        )
         return (weights_new, first_new, second_new, copies, ratios)
 
     return shards

time: 149 us -> 171 us (1.15)
  blocking collectives: 53.1 us -> 116 us
  waiting for transfers between devices: 54.1 us -> 16.2 us
  between operations: 14.1 us -> 0.73 us
  local copies, waits for them, and re-layouts: 7.68 us -> 18.1 us
    all_to_all x0 -> x1, blocking collectives: none -> 62.9 us  [shards(): lax.all_to_all(jnp.stack([weights_new.astype(jnp.bfloat16)] * lax.axis_si...]
    all_gather x1 -> x0, waiting for transfers between devices: 38 us -> none  [shards(): lax.all_gather(weights_new.astype(jnp.bfloat16), TN, axis=1, tiled=True)]
    reshape x0 -> x1, local copies, waits for them, and re-layouts: none -> 7.41 us  [shards(): jnp.concatenate(lax.all_to_all(jnp.stack([weights_new.astype(jnp.bfloat16...]
    unnamed x5, local copies, waits for them, and re-layouts: 5.13 us -> 7.52 us
  transfers between devices with their start and end apart: 5 -> 4, of which waited for: 5 -> 4; matrix products, arithmetic and copies ran while one was open for 0% -> 0% of each run, Pallas kernels for 0% -> 0%
where the time goes in v1:
time: 171 us
  blocking collectives  116 us (68%)
  local copies, waits for them, and re-layouts  18.1 us (11%)
  waiting for transfers between devices  16.2 us (9%)
  starting transfers between devices  13.4 us (8%)
  other arithmetic  5.86 us (3%)
    all_to_all x1, blocking collectives, shards(): lax.all_to_all(jnp.stack([weights_new.astype(jnp.bfloat16)] * lax.axis_si...  62.9 us
    all_to_all x1, blocking collectives, dp_sum(): lax.all_to_all(y.reshape(nx, padded // nx, cols), 'x', 0, 0, tiled=False)  21.6 us
    all_to_all x1, blocking collectives, dp_sum(): lax.all_to_all(y.reshape(nz, padded // (nx * nz), cols), 'z', 0, 0, tiled...  18.7 us
    all_to_all x1, waiting for transfers between devices, dp_sum(): lax.all_to_all(jnp.broadcast_to(y[None], (nx,) + y.shape), 'x', 0, 0, til...  13.2 us
    all_to_all x1, blocking collectives, dp_sum(): lax.all_to_all(jnp.broadcast_to(y[None], (nz,) + y.shape), 'z', 0, 0, til...  12.8 us
    ppermute x3, starting transfers between devices, tensor_sum(): v = v + lax.ppermute(v, axis, [(i, i ^ step) for i in range(size)])  9.76 us
    unnamed x5, local copies, waits for them, and re-layouts  7.52 us
    reshape x1, local copies, waits for them, and re-layouts, shards(): jnp.concatenate(lax.all_to_all(jnp.stack([weights_new.astype(jnp.bfloat16...  7.41 us
  transfers between devices with their start and end apart: 4, of which 4 were waited for; matrix products, arithmetic and copies ran while one was open for 0% of the time, Pallas kernels for 0%

profile of v1, /device:TPU:1, one launch (start us, length us, event | category | flops | bytes accessed | tf_op | source)
XLA Modules:
  0.0 170.8 jit_solution(8291064784099711477)
XLA Ops:
  0.6 1.4 pad.4
  2.0 21.6 %all_to_all.25 = f32[4,640,128]{2,1,0:T(8,128)S(1)} all-to-all(f32[4,640,128]{2,1,0:T(8,128)S(1)} %bitcast.21), channel_id=1, replica_groups=mesh['z'=8,'x'=4,'y'=4,'core'=2] {'x'}, dimensions={0} | all-to-all | bytes 2621440 | tf_op jit(solution)/shard_map/all_to_all | solution.py:55
  23.6 0.1 reduce_sum.37
  23.7 18.7 %all_to_all.26 = f32[8,80,128]{2,1,0:T(8,128)S(1)} all-to-all(f32[8,80,128]{2,1,0:T(8,128)S(1)} %bitcast.23), channel_id=1, replica_groups=mesh['z'=8,'x'=4,'y'=4,'core'=2] {'z'}, dimensions={0} | all-to-all | bytes 655360 | tf_op jit(solution)/shard_map/all_to_all | solution.py:56
  42.4 12.8 %all_to_all.27 = f32[8,80,128]{2,1,0:T(8,128)S(1)} all-to-all(f32[8,80,128]{2,1,0:T(8,128)S(1)} %broadcast_in_dim.24), channel_id=1, replica_groups=mesh['z'=8,'x'=4,'y'=4,'core'=2] {'z'}, dimensions={0} | all-to-all | bytes 655360 | tf_op jit(solution)/shard_map/all_to_all | solution.py:57
  55.3 1.1 broadcast_in_dim.26
  56.4 0.0 copy-start
  56.4 3.7 %all-to-all-start.3 = ((f32[4,640,128]{2,1,0:T(8,128)}), f32[4,640,128]{2,1,0:T(8,128)S(1)}, u32[]{:S(2)}, u32[]{:S(2)}) async-start(f32[4,640,128]{2,1,0:T(8,128)} %broadcast_in_dim.26), calls=%async_computation.3 | async-start | bytes 2621440 | tf_op jit(solution)/shard_map/all_to_all | solution.py:59
  60.2 13.2 %all-to-all-done.3 = f32[4,640,128]{2,1,0:T(8,128)S(1)} async-done(((f32[4,640,128]{2,1,0:T(8,128)}), f32[4,640,128]{2,1,0:T(8,128)S(1)}, u32[]{:S(2)}, u32[]{:S(2)}) %all-to-all-start.3) | async-done | bytes 1310752 | tf_op jit(solution)/shard_map/all_to_all | solution.py:59
  73.4 0.0 copy-done
  73.4 4.0 %multiply_reduce_fusion = (f32[2368]{0:T(1024)S(1)}, f32[2368,128]{1,0:T(8,128)S(1)}, f32[2368,128]{1,0:T(8,128)}, f32[2368,128]{1,0:T(8,128)}, f32[2368]{0:T(1024)S(1)}) fusion(f32[2368,128]{1,0:T(8,128)S(1)} %copy-done, f32[2368]{0:T(1024)S(1)} %fusion.1, f32[2560,128]{1,0:T(8,128)S(1)} %bitcast.22, f32[2368,128]{1,0:T(8,128)} %param.6, f32[2368,128]{1,0:T(8,128)} %param.7), kind=kLoop, calls=%fused_computation.1 | loop fusion | flops 5451136 | bytes 8515328 | tf_op jit(solution)/shard_map/reduce_sum | solution.py:29
  77.4 0.1 convolution_bitcast_fusion
  77.5 0.2 convolution_bitcast_fusion.1
  77.7 0.1 pad_maximum_fusion
  77.9 5.5 %collective-permute-start = (f32[8]{0:T(128)S(1)}, f32[8]{0:T(128)S(1)}, u32[]{:S(2)}, u32[]{:S(2)}) collective-permute-start(f32[8]{0:T(128)S(1)} %pad_maximum_fusion), channel_id=1, source_target_pairs={{0,1},{1,0},{2,3},{3,2},{4,5},{5,4},{6,7},{7,6},{8,9},{9,8},{10,11... | collective-permute-start | bytes 104 | tf_op jit(solution)/shard_map/ppermute | solution.py:67
  83.4 0.8 collective-permute-done
  84.2 0.1 fusion.10
  84.3 1.3 collective-permute-start.1
  85.6 1.1 collective-permute-done.1
  86.7 2.9 %collective-permute-start.2 = (f32[8]{0:T(128)S(1)}, f32[8]{0:T(128)S(1)}, u32[]{:S(2)}, u32[]{:S(2)}) collective-permute-start(f32[8]{0:T(128)S(1)} %add.59), channel_id=1, source_target_pairs={{0,4},{2,6},{4,0},{6,2},{1,5},{3,7},{5,1},{7,3},{8,12},{10,14},{12... | collective-permute-start | bytes 104 | tf_op jit(solution)/shard_map/ppermute | solution.py:67
  89.6 1.0 collective-permute-done.2
  90.7 0.1 rsqrt_multiply_fusion
  90.7 0.0 copy-start.1
  90.7 0.2 convolution_reduce_fusion
  90.9 1.4 fusion.3
  92.4 0.0 copy-done.1
  92.4 0.6 stack.2
  93.0 62.9 %all_to_all.28 = bf16[8,2368,128]{2,1,0:T(8,128)(2,1)} all-to-all(bf16[8,2368,128]{2,1,0:T(8,128)(2,1)S(1)} %stack.2), channel_id=1, replica_groups=mesh['z'=8,'x'=4,'y'=4,'core'=2] {'y','core'}, dimensions={0} | all-to-all | bytes 9699328 | tf_op jit(solution)/shard_map/all_to_all | solution.py:89
  155.8 7.4 %copy.11 = bf16[2368,8,128]{0,2,1:T(8,128)(2,1)} copy(bf16[2368,8,128]{2,0,1:T(8,128)(2,1)} %bitcast.20) | data formatting | bytes 9699328 | tf_op jit(solution)/shard_map/reshape | solution.py:88
  163.3 7.5 %copy.12 = bf16[2368,1024]{1,0:T(8,128)(2,1)} copy(bf16[2368,1024]{0,1:T(8,128)(2,1)} %bitcast.19) | data formatting | bytes 9699328
  (11 shorter events, 0.2 us)
Async XLA Ops:
  56.4 17.0 %copy-start = (f32[2368,128]{1,0:T(8,128)S(1)}, f32[2368,128]{1,0:T(8,128)}, u32[]{:S(2)}) copy-start(f32[2368,128]{1,0:T(8,128)} %param.5) | copy-start | bytes 3637252
  56.4 17.0 %all-to-all-start.3 = ((f32[4,640,128]{2,1,0:T(8,128)}), f32[4,640,128]{2,1,0:T(8,128)S(1)}, u32[]{:S(2)}, u32[]{:S(2)}) async-start(f32[4,640,128]{2,1,0:T(8,128)} %broadcast_in_dim.26), calls=%async_computation.3 | async-start | bytes 2621440 | tf_op jit(solution)/shard_map/all_to_all | solution.py:59
  77.9 6.4 %collective-permute-start = (f32[8]{0:T(128)S(1)}, f32[8]{0:T(128)S(1)}, u32[]{:S(2)}, u32[]{:S(2)}) collective-permute-start(f32[8]{0:T(128)S(1)} %pad_maximum_fusion), channel_id=1, source_target_pairs={{0,1},{1,0},{2,3},{3,2},{4,5},{5,4},{6,7},{7,6},{8,9},{9,8},{10,11... | collective-permute-start | bytes 104 | tf_op jit(solution)/shard_map/ppermute | solution.py:67
  84.3 2.4 %collective-permute-start.1 = (f32[8]{0:T(128)S(1)}, f32[8]{0:T(128)S(1)}, u32[]{:S(2)}, u32[]{:S(2)}) collective-permute-start(f32[8]{0:T(128)S(1)} %fusion.10), channel_id=1, source_target_pairs={{0,2},{2,0},{4,6},{6,4},{1,3},{3,1},{5,7},{7,5},{8,10},{10,8},{12,... | collective-permute-start | bytes 104 | tf_op jit(solution)/shard_map/ppermute | solution.py:67
  86.7 3.9 %collective-permute-start.2 = (f32[8]{0:T(128)S(1)}, f32[8]{0:T(128)S(1)}, u32[]{:S(2)}, u32[]{:S(2)}) collective-permute-start(f32[8]{0:T(128)S(1)} %add.59), channel_id=1, source_target_pairs={{0,4},{2,6},{4,0},{6,2},{1,5},{3,7},{5,1},{7,3},{8,12},{10,14},{12... | collective-permute-start | bytes 104 | tf_op jit(solution)/shard_map/ppermute | solution.py:67
  90.7 1.6 copy-start.1
